TPU v7x, 256 devices: a whole 4x4x8 slice. The times are simulated.
256 devices in a mesh: grid: 16 (over y_hi, z), states: 16 (over y_lo, x, core).
Axes of the slice: x: 4, y: 4 (y_hi: 2, y_lo: 2; y = y_hi * 2 + y_lo), z: 8, core: 2. Of those that a mesh axis runs over, the one named last changes fastest.
Arguments:
- states_in: float32 [16, 256, 32, 128], P('states', 'grid'), may hold values from -10 to 10
- potential: float32 [256, 32, 128], P('grid'), may hold values from -2 to 0.5
- projectors: bfloat16 [16, 32, 8, 4096], P('grid', 'states'), may hold values from -0.0625 to 0.0625
- proj_gains: bfloat16 [16, 32, 8], P('grid', 'states'), may hold values from 1 to 6
- atom_owner: int32 [160], P('grid'), may hold values from 0 to 15, as said below
- atom_rows: int32 [160, 32], P('grid'), may hold values from -1 to 8191, as said below
- wrap_rows: int32 [32], replicated, may hold values from 0 to 31, as said below
Outputs:
- filtered: float32 [16, 256, 32, 128], P('states', 'grid')
Inputs may be any that keep to these rules, and one draw needn't show every extreme that they name: `atom_owner`: atom a belongs to tile a // 10. At most 2 atoms of one tile share an owner, and one owner takes exactly 2 atoms of every tile. `atom_rows`: A row r is the line of cells at x = r // 32, y = r % 32. Each list holds distinct rows whose x lies in the atom's own tile of 16 planes, followed by -1 entries; each list has 16 rows or more, and the first atom of every tile fills all 32. wrap_rows[y] = (y + t) mod 32 for one t of 1 to 31.
All inputs are finite; a program needn't handle non-finite values.
Results may differ from a plain program's by a relative error of at most 0.00082.
Values may be sent and summed in bfloat16 or wider, within the bound.
No kernel may reach another device: no remote copies, remote signals or barrier semaphores. Data moves between devices by JAX's collectives and lax.ppermute only.
A program may use at most 64 MiB of HBM per device.

v0:
```python
import math
import jax
import jax.numpy as jnp
from jax import lax
from jax.sharding import PartitionSpec as P

RADIUS = 6
PAIR_CAP = 2
MIXED_WEIGHT = 0.7
CENTER = 12.0
HALF_WIDTH = 8.0


def padded_2(shard, sides, width):
    for axis, dim in sides:
        count, length = (lax.axis_size(axis), shard.shape[dim])
        up = [(i, (i + 1) % count) for i in range(count)]
        down = [(j, i) for i, j in up]
        last = lax.slice_in_dim(shard, length - width, length, axis=dim)
        initial = lax.slice_in_dim(shard, 0, width, axis=dim)
        before = lax.ppermute(last, axis, up)
        after = lax.ppermute(initial, axis, down)
        shard = jnp.concatenate([before, shard, after], axis=dim)
    return shard


def second_table(radius):
    weights = [-2.0 * sum((1.0 / (k * k) for k in range(1, radius + 1)))]
    for k in range(1, radius + 1):
        weights.append(
            2.0
            * (-1) ** (k + 1)
            * math.factorial(radius) ** 2
            / (k * k * math.factorial(radius - k) * math.factorial(radius + k))
        )
    return weights


def first_table(radius):
    weights = [0.0]
    for k in range(1, radius + 1):
        weights.append(
            (-1) ** (k + 1)
            * math.factorial(radius) ** 2
            / (k * math.factorial(radius - k) * math.factorial(radius + k))
        )
    return weights


def laplacian(padded, plane_count):
    second_weights = second_table(RADIUS)
    first_weights = first_table(RADIUS)
    interior = padded[:, RADIUS : RADIUS + plane_count]
    line_depth = interior.shape[3]
    z_padded = jnp.pad(interior, ((0, 0), (0, 0), (0, 0), (RADIUS, RADIUS)))
    summed = 3.0 * second_weights[0] * interior
    y_slope = jnp.zeros_like(padded)
    for k in range(1, RADIUS + 1):
        summed = summed + second_weights[k] * (
            padded[:, RADIUS + k : RADIUS + k + plane_count]
            + padded[:, RADIUS - k : RADIUS - k + plane_count]
        )
        summed = summed + second_weights[k] * (jnp.roll(interior, -k, 2) + jnp.roll(interior, k, 2))
        summed = summed + second_weights[k] * (
            z_padded[:, :, :, RADIUS + k : RADIUS + k + line_depth]
            + z_padded[:, :, :, RADIUS - k : RADIUS - k + line_depth]
        )
        y_slope = y_slope + first_weights[k] * (jnp.roll(padded, -k, 2) - jnp.roll(padded, k, 2))
    cross_term = jnp.zeros_like(interior)
    for k in range(1, RADIUS + 1):
        cross_term = cross_term + first_weights[k] * (
            y_slope[:, RADIUS + k : RADIUS + k + plane_count]
            - y_slope[:, RADIUS - k : RADIUS - k + plane_count]
        )
    return summed + MIXED_WEIGHT * cross_term


def shards(states_in, potential, projectors, proj_gains, atom_owner, atom_rows, wrap_rows):
    state_count, tile_width, breadth, line_depth = states_in.shape
    n_grid = lax.axis_size("grid")
    n_states = lax.axis_size("states")
    tile_index = lax.axis_index("grid")
    tile_lines = tile_width * breadth
    block_rows = atom_rows.shape[1]
    line_span = block_rows * line_depth
    proj_count = projectors.shape[2]
    home_count = atom_owner.shape[0]
    slot_pairs = projectors.shape[1]
    row_order = jnp.arange(breadth, dtype=jnp.int32)
    unwrap_rows = jnp.sum(
        row_order[None, :] * (wrap_rows[None, :] == row_order[:, None]).astype(jnp.int32), axis=1
    )
    atom_order = jnp.arange(home_count, dtype=jnp.int32)
    same_owner = (atom_owner[:, None] == atom_owner[None, :]) & (
        atom_order[None, :] < atom_order[:, None]
    )
    owner_rank = jnp.sum(same_owner.astype(jnp.int32), axis=1)
    atom_slot = atom_owner * PAIR_CAP + owner_rank
    local_rows = jnp.where(atom_rows >= 0, atom_rows - tile_index * tile_lines, tile_lines)
    gain_lanes = jnp.zeros((1, slot_pairs, proj_count, 128), jnp.bfloat16)
    gain_lanes = gain_lanes.at[..., 0].set(proj_gains)
    packed = jnp.concatenate([projectors, gain_lanes], axis=3)
    pairs = [(o * n_states + t, t * n_states + o) for o in range(n_grid) for t in range(n_states)]
    packed = lax.ppermute(packed, ("grid", "states"), pairs)
    gathered = lax.all_gather(packed[0], "states", axis=0, tiled=True)
    gathered = gathered.reshape(n_states * slot_pairs, proj_count, line_span + 128)
    atom_pack = jnp.take(gathered, atom_slot, axis=0)
    proj_rows = atom_pack[:, :, :line_span].reshape(home_count * proj_count, line_span)
    atom_gain = atom_pack[:, :, line_span].astype(jnp.float32)
    selector = (
        local_rows.reshape(-1)[:, None] == jnp.arange(tile_lines, dtype=jnp.int32)[None, :]
    ).astype(jnp.bfloat16)
    atom_eye = jnp.eye(home_count, dtype=jnp.float32)

    def extended(grid_field):
        padded = padded_2(grid_field, (("grid", 1),), RADIUS)
        low_rim = padded[:, :RADIUS]
        high_rim = padded[:, RADIUS + tile_width :]
        low_rim = jnp.where(tile_index == 0, jnp.take(low_rim, wrap_rows, axis=2), low_rim)
        high_rim = jnp.where(
            tile_index == n_grid - 1, jnp.take(high_rim, unwrap_rows, axis=2), high_rim
        )
        return jnp.concatenate([low_rim, padded[:, RADIUS : RADIUS + tile_width], high_rim], axis=1)

    def nonlocal_part(grid_field):
        lines_here = grid_field.reshape(tile_lines, line_depth).astype(jnp.bfloat16)
        picked = jnp.dot(selector, lines_here, preferred_element_type=jnp.float32)
        picked = picked.astype(jnp.bfloat16).reshape(home_count, line_span)
        every_pair = lax.dot_general(
            proj_rows, picked, (((1,), (1,)), ((), ())), preferred_element_type=jnp.float32
        ).reshape(home_count, proj_count, home_count)
        coefficients = jnp.sum(every_pair * atom_eye[:, None, :], axis=2)
        scaled = (coefficients * atom_gain).astype(jnp.bfloat16)
        block_scaled = (atom_eye.astype(jnp.bfloat16)[:, :, None] * scaled[None, :, :]).reshape(
            home_count, home_count * proj_count
        )
        projected = jnp.dot(block_scaled, proj_rows, preferred_element_type=jnp.float32)
        projected = projected.astype(jnp.bfloat16).reshape(home_count * block_rows, line_depth)
        summed = lax.dot_general(
            selector, projected, (((0,), (0,)), ((), ())), preferred_element_type=jnp.float32
        )
        return summed.reshape(state_count, tile_width, breadth, line_depth)

    def operate(grid_field):
        padded = extended(grid_field)
        return (
            -0.5 * laplacian(padded, tile_width)
            + potential[None] * grid_field
            + nonlocal_part(grid_field)
        )

    def shifted(grid_field):
        return (operate(grid_field) - CENTER * grid_field) / HALF_WIDTH

    first_term = shifted(states_in)
    second_term = 2.0 * shifted(first_term) - states_in
    return 2.0 * shifted(second_term) - first_term


def solution(mesh):
    in_specs = (
        P("states", "grid", None, None),
        P("grid", None, None),
        P("grid", "states", None, None),
        P("grid", "states", None),
        P("grid"),
        P("grid", None),
        P(),
    )
    out_specs = P("states", "grid", None, None)
    return jax.shard_map(shards, mesh=mesh, in_specs=in_specs, out_specs=out_specs, check_vma=False)
```

profile of v0, /device:TPU:2, one launch (start us, length us, event | category | flops | bytes accessed | tf_op | source)
XLA Modules:
  0.0 135.8 jit_solution(8653599819950323269)
XLA Ops:
  6.5 0.8 copy.55
  7.3 0.9 fusion.328
  8.3 5.2 %collective-permute-start.2 = (bf16[1,2,8,4224]{3,2,0,1:T(8,128)(2,1)S(1)}, bf16[1,2,8,4224]{3,2,0,1:T(8,128)(2,1)S(1)}, u32[]{:S(2)}, u32[]{:S(2)}) collective-permute-start(bf16[1,2,8,4224]{3,2,0,1:T(8,128)(2,1)S(1)} %fusion.328), channel_id=1, source_target_pairs={{0,0},{1,16},{2,32},{3,48},{4,64},{5,80},{6,96},{7,112},{8,128},{9... | collective-permute-start | bytes 405512 | tf_op jit(solution)/shard_map/ppermute | solution.py:104
  13.4 1.0 fusion.419
  14.4 6.3 %collective-permute-start = (f32[1,6,32,128]{3,2,1,0:T(8,128)S(1)}, f32[1,6,32,128]{3,2,1,0:T(8,128)S(1)}, u32[]{:S(2)}, u32[]{:S(2)}) collective-permute-start(f32[1,6,32,128]{3,2,1,0:T(8,128)S(1)} %get-tuple-element.164), channel_id=1, source_target_pairs={{16,0},{32,16},{48,32},{64,48},{80,64},{96,80},{112,96},{128,112},... | collective-permute-start | bytes 294920 | tf_op jit(solution)/shard_map/ppermute | solution.py:22
  20.7 1.0 convert_element_type.119
  21.7 0.6 fusion.344
  22.5 0.6 fusion.407
  23.1 0.7 fusion.410
  23.9 0.8 fusion.412
  24.7 0.6 fusion.411
  25.4 0.8 fusion.414
  26.2 0.6 fusion.413
  26.8 0.9 fusion.416
  27.7 0.6 fusion.415
  28.3 0.6 fusion.417
  29.1 0.6 compare_and_fusion.2
  30.1 0.7 copy-done.16
  30.8 0.7 reshape.2360
  31.5 0.7 copy.43
  32.2 0.7 fusion.409
  32.9 0.8 fusion.418
  34.5 0.6 gather_fusion.2
  36.0 0.8 fusion.76
  36.8 30.0 %all-gather.3.cloned.1.call-done = bf16[1,32,8,4224]{3,2,0,1:T(8,128)(2,1)} async-done(((bf16[1,2,8,4224]{3,2,0,1:T(8,128)(2,1)}), bf16[1,32,8,4224]{3,2,0,1:T(8,128)(2,1)}) %all-gather.3.cloned.1.call-update) | async-done | bytes 2162704 | tf_op jit(solution)/shard_map/all_gather | solution.py:105
  66.8 2.2 %gather_fusion = bf16[10,8,4224]{2,1,0:T(8,128)(2,1)S(1)} fusion(bf16[32,8,4224]{2,1,0:T(8,128)(2,1)} %bitcast.111, s32[1024]{0:T(1024)S(1)} %pad_clamp_fusion), kind=kCustom, calls=%fused_computation.6 | custom fusion | bytes 1351720 | tf_op jit(solution)/shard_map/jit(_take)/gather | solution.py:107
  69.1 0.9 copy_select_fusion
  70.1 1.3 fusion.48
  72.5 4.3 %broadcast_multiply_fusion = (f32[1,16,32,128]{3,2,1,0:T(8,128)S(1)}, bf16[1,16,32,128]{3,2,1,0:T(8,128)(2,1)S(1)}, f32[1,16,32,128]{3,2,1,0:T(8,128)}) fusion(f32[1,16,32,128]{3,2,1,0:T(8,128)S(1)} %copy-done, bf16[320,128,1]{1,0,2:T(8,128)(2,1)S(1)} %reshape.2362, s32[16,32]{1,0:T(8,128)S(1)} %multiply_add_fusion, s32[320]{0:T(512)} %copy-done.55, ...), kind=kOutput, calls=%fused_computation.493 | convolution fusion | flops 49053696 | bytes 7752960 | tf_op jit(solution)/shard_map/dot_general | solution.py:139
  76.9 0.7 fusion.394
  77.6 0.7 fusion.396
  78.2 0.7 fusion.399
  79.0 0.6 fusion.398
  79.6 0.8 fusion.401
  80.5 0.6 fusion.400
  81.1 0.8 fusion.403
  81.9 0.8 fusion.405
  83.1 1.3 fusion.49
  85.0 5.6 %collective-permute-start.3 = (f32[1,6,32,128]{3,2,1,0:T(8,128)S(1)}, f32[1,6,32,128]{3,2,1,0:T(8,128)S(1)}, u32[]{:S(2)}, u32[]{:S(2)}) collective-permute-start(f32[1,6,32,128]{3,2,1,0:T(8,128)S(1)} %get-tuple-element.136), channel_id=1, source_target_pairs={{16,0},{32,16},{48,32},{64,48},{80,64},{96,80},{112,96},{128,112},... | collective-permute-start | bytes 294920 | tf_op jit(solution)/shard_map/ppermute | solution.py:22
  90.6 0.6 fusion.404
  91.2 0.7 reshape.2365
  91.9 1.1 collective-permute-done.3
  93.7 5.2 %collective-permute-done.4 = f32[1,6,32,128]{3,2,1,0:T(8,128)S(1)} collective-permute-done((f32[1,6,32,128]{3,2,1,0:T(8,128)S(1)}, f32[1,6,32,128]{3,2,1,0:T(8,128)S(1)}, u32[]{:S(2)}, u32[]{:S(2)}) %collective-permute-start.4) | collective-permute-done | bytes 98336 | tf_op jit(solution)/shard_map/ppermute | solution.py:21
  98.9 0.7 gather_fusion.4
  99.6 0.8 fusion.332
  100.4 0.7 fusion.331
  102.0 0.8 fusion.67
  103.6 1.4 %fusion.420 = (bf16[1,16,32,128]{3,2,1,0:T(8,128)(2,1)S(1)}, f32[1,16,32,128]{3,2,1,0:T(8,128)S(1)}) fusion(f32[1,16,32,128]{3,2,1,0:T(8,128)S(1)} %copy-done, f32[1,16,32,128]{3,2,1,0:T(8,128)S(1)} %copy-done.63, bf16[320,128,1]{1,0,2:T(8,128)(2,1)S(1)} %copy-done.18, s32[16,32]{1,0:T(8,128)S(1)} %multiply_add_fusion, s32[320]{0:T(512)S(1)} %copy-done.57, ...), kind=kOutput, calls=%fused_computation.611 | convolution fusion | flops 49119232 | bytes 8015104 | tf_op jit(solution)/shard_map/dot_general | solution.py:139
  105.1 0.6 fusion.389
  105.7 0.6 fusion.387
  106.4 0.7 fusion.388
  107.1 0.6 fusion.385
  107.8 0.8 fusion.386
  108.6 0.7 fusion.383
  109.3 0.8 fusion.384
  110.1 0.7 fusion.381
  110.8 0.8 fusion.382
  112.0 1.3 fusion.50
  113.9 5.6 %collective-permute-start.5 = (f32[1,6,32,128]{3,2,1,0:T(8,128)S(1)}, f32[1,6,32,128]{3,2,1,0:T(8,128)S(1)}, u32[]{:S(2)}, u32[]{:S(2)}) collective-permute-start(f32[1,6,32,128]{3,2,1,0:T(8,128)S(1)} %get-tuple-element.110), channel_id=1, source_target_pairs={{16,0},{32,16},{48,32},{64,48},{80,64},{96,80},{112,96},{128,112},... | collective-permute-start | bytes 294920 | tf_op jit(solution)/shard_map/ppermute | solution.py:22
  119.5 0.6 fusion.391
  120.2 1.9 %collective-permute-done.6 = f32[1,6,32,128]{3,2,1,0:T(8,128)S(1)} collective-permute-done((f32[1,6,32,128]{3,2,1,0:T(8,128)S(1)}, f32[1,6,32,128]{3,2,1,0:T(8,128)S(1)}, u32[]{:S(2)}, u32[]{:S(2)}) %collective-permute-start.6) | collective-permute-done | bytes 98336 | tf_op jit(solution)/shard_map/ppermute | solution.py:21
  122.2 0.7 gather_fusion.6
  124.6 0.8 fusion.58
  126.2 2.7 %fusion.27 = f32[1,16,32,128]{3,2,1,0:T(8,128)} fusion(bf16[320,128,1]{1,0,2:T(8,128)(2,1)S(1)} %reshape.2368, s32[16,32]{1,0:T(8,128)S(1)} %multiply_add_fusion, s32[320]{0:T(512)S(1)} %copy-done.58, f32[1,16,32,128]{3,2,1,0:T(8,128)S(1)} %get-tuple-element.168, f32[1,6,32,128]{3,2,1,0:T(8,128)S(1)} %fusion.329, f32[1,6,32,128]{3,2,1,0:T(8,128)S(1)} %fusion.330, ...), kind=kOutput, calls=%fused_computation.61 | convolution fusion | flops 49119232 | bytes 7621888 | tf_op jit(solution)/shard_map/dot_general | solution.py:139
  (222 shorter events, 9.5 us)
Async XLA Ops:
  6.5 15.9 %copy-start = (f32[1,16,32,128]{3,2,1,0:T(8,128)S(1)}, f32[1,16,32,128]{3,2,1,0:T(8,128)}, u32[]{:S(2)}) copy-start(f32[1,16,32,128]{3,2,1,0:T(8,128)} %param.11) | copy-start | bytes 786436
  6.5 15.7 %copy-start.62 = (s32[32]{0:T(128)S(1)}, s32[32]{0:T(128)}, u32[]{:S(2)}) copy-start(s32[32]{0:T(128)} %param.17) | copy-start | bytes 388
  6.5 60.3 %all-gather.3.cloned.1.call-start = ((), (), s32[]{:S(2)}) async-start(), calls=%async_computation | async-start | bytes 2297856 | tf_op jit(solution)/shard_map/all_gather | solution.py:105
  8.3 21.9 %collective-permute-start.2 = (bf16[1,2,8,4224]{3,2,0,1:T(8,128)(2,1)S(1)}, bf16[1,2,8,4224]{3,2,0,1:T(8,128)(2,1)S(1)}, u32[]{:S(2)}, u32[]{:S(2)}) collective-permute-start(bf16[1,2,8,4224]{3,2,0,1:T(8,128)(2,1)S(1)} %fusion.328), channel_id=1, source_target_pairs={{0,0},{1,16},{2,32},{3,48},{4,64},{5,80},{6,96},{7,112},{8,128},{9... | collective-permute-start | bytes 405512 | tf_op jit(solution)/shard_map/ppermute | solution.py:104
  14.4 19.3 %collective-permute-start = (f32[1,6,32,128]{3,2,1,0:T(8,128)S(1)}, f32[1,6,32,128]{3,2,1,0:T(8,128)S(1)}, u32[]{:S(2)}, u32[]{:S(2)}) collective-permute-start(f32[1,6,32,128]{3,2,1,0:T(8,128)S(1)} %get-tuple-element.164), channel_id=1, source_target_pairs={{16,0},{32,16},{48,32},{64,48},{80,64},{96,80},{112,96},{128,112},... | collective-permute-start | bytes 294920 | tf_op jit(solution)/shard_map/ppermute | solution.py:22
  20.7 13.1 %collective-permute-start.1 = (f32[1,6,32,128]{3,2,1,0:T(8,128)S(1)}, f32[1,6,32,128]{3,2,1,0:T(8,128)S(1)}, u32[]{:S(2)}, u32[]{:S(2)}) collective-permute-start(f32[1,6,32,128]{3,2,1,0:T(8,128)S(1)} %get-tuple-element.165), channel_id=1, source_target_pairs={{0,16},{16,32},{32,48},{48,64},{64,80},{80,96},{96,112},{112,128},... | collective-permute-start | bytes 294920 | tf_op jit(solution)/shard_map/ppermute | solution.py:21
  22.4 12.7 %copy-start.48 = (pred[32]{0:T(512)(128)(4,1)}, pred[32]{0:T(512)(128)(4,1)S(1)}, u32[]{:S(2)}) copy-start(pred[32]{0:T(512)(128)(4,1)S(1)} %compare_and_fusion.1) | copy-start | bytes 100
  22.5 12.7 %copy-start.50 = (pred[32]{0:T(512)(128)(4,1)}, pred[32]{0:T(512)(128)(4,1)S(1)}, u32[]{:S(2)}) copy-start(pred[32]{0:T(512)(128)(4,1)S(1)} %compare_and_fusion) | copy-start | bytes 100
  25.4 3.5 %copy-start.59 = (s32[10]{0:T(128)S(1)}, s32[10]{0:T(128)}, u32[]{:S(2)}) copy-start(s32[10]{0:T(128)} %param.15) | copy-start | bytes 124
  25.4 4.3 %copy-start.38 = (s32[10,32]{1,0:T(8,128)S(1)}, s32[10,32]{1,0:T(8,128)}, u32[]{:S(2)}) copy-start(s32[10,32]{1,0:T(8,128)} %param.16) | copy-start | bytes 3844
  29.8 4.0 %copy-start.55 = (s32[320]{0:T(512)}, s32[320]{0:T(512)S(1)}, u32[]{:S(2)}) copy-start(s32[320]{0:T(512)S(1)} %eq.101) | copy-start | bytes 3844
  33.7 1.5 %copy-start.47 = (s32[1024]{0:T(1024)}, s32[1024]{0:T(1024)S(1)}, u32[]{:S(2)}) copy-start(s32[1024]{0:T(1024)S(1)} %pad_clamp_fusion.1) | copy-start | bytes 12292
  69.1 1.1 copy-start.17
  69.1 1.1 copy-start.39
  70.0 1.5 %copy-start.52 = (bf16[10,10]{1,0:T(8,128)(2,1)S(1)}, bf16[10,10]{1,0:T(8,128)(2,1)}, u32[]{:S(2)}) copy-start(bf16[10,10]{1,0:T(8,128)(2,1)} %copy.43) | copy-start | bytes 604
  81.1 1.7 %copy-start.56 = (s32[320]{0:T(512)S(1)}, s32[320]{0:T(512)}, u32[]{:S(2)}) copy-start(s32[320]{0:T(512)} %copy-done.55) | copy-start | bytes 3844
  81.9 1.2 copy-start.40
  83.1 1.5 %copy-start.53 = (bf16[10,10]{1,0:T(8,128)(2,1)S(1)}, bf16[10,10]{1,0:T(8,128)(2,1)}, u32[]{:S(2)}) copy-start(bf16[10,10]{1,0:T(8,128)(2,1)} %copy.43) | copy-start | bytes 604
  85.0 8.0 %collective-permute-start.3 = (f32[1,6,32,128]{3,2,1,0:T(8,128)S(1)}, f32[1,6,32,128]{3,2,1,0:T(8,128)S(1)}, u32[]{:S(2)}, u32[]{:S(2)}) collective-permute-start(f32[1,6,32,128]{3,2,1,0:T(8,128)S(1)} %get-tuple-element.136), channel_id=1, source_target_pairs={{16,0},{32,16},{48,32},{64,48},{80,64},{96,80},{112,96},{128,112},... | collective-permute-start | bytes 294920 | tf_op jit(solution)/shard_map/ppermute | solution.py:22
  90.6 8.3 %collective-permute-start.4 = (f32[1,6,32,128]{3,2,1,0:T(8,128)S(1)}, f32[1,6,32,128]{3,2,1,0:T(8,128)S(1)}, u32[]{:S(2)}, u32[]{:S(2)}) collective-permute-start(f32[1,6,32,128]{3,2,1,0:T(8,128)S(1)} %get-tuple-element.137), channel_id=1, source_target_pairs={{0,16},{16,32},{32,48},{48,64},{64,80},{80,96},{96,112},{112,128},... | collective-permute-start | bytes 294920 | tf_op jit(solution)/shard_map/ppermute | solution.py:21
  101.8 1.0 copy-start.9
  101.8 1.1 copy-start.11
  101.8 1.2 copy-start.12
  101.8 1.2 copy-start.13
  101.8 1.3 copy-start.14
  101.9 1.4 %copy-start.15 = (f32[1,16,31,128]{3,2,1,0:T(8,128)S(1)}, f32[1,16,31,128]{3,2,1,0:T(8,128)}, u32[]{:S(2)}) copy-start(f32[1,16,31,128]{3,2,1,0:T(8,128)} %get-tuple-element.135) | copy-start | bytes 761860
  101.9 1.4 %copy-start.18 = (bf16[320,128,1]{1,0,2:T(8,128)(2,1)S(1)}, bf16[320,128,1]{1,0,2:T(8,128)(2,1)}, u32[]{:S(2)}) copy-start(bf16[320,128,1]{1,0,2:T(8,128)(2,1)} %reshape.2365) | copy-start | bytes 245764
  101.9 1.4 %copy-start.23 = (f32[1,16,6,128]{3,2,1,0:T(8,128)S(1)}, f32[1,16,6,128]{3,2,1,0:T(8,128)}, u32[]{:S(2)}) copy-start(f32[1,16,6,128]{3,2,1,0:T(8,128)} %get-tuple-element.112) | copy-start | bytes 147460
  101.9 1.4 %copy-start.24 = (f32[1,16,6,128]{3,2,1,0:T(8,128)S(1)}, f32[1,16,6,128]{3,2,1,0:T(8,128)}, u32[]{:S(2)}) copy-start(f32[1,16,6,128]{3,2,1,0:T(8,128)} %get-tuple-element.113) | copy-start | bytes 147460
  101.9 1.4 %copy-start.25 = (f32[1,16,5,128]{3,2,1,0:T(8,128)S(1)}, f32[1,16,5,128]{3,2,1,0:T(8,128)}, u32[]{:S(2)}) copy-start(f32[1,16,5,128]{3,2,1,0:T(8,128)} %get-tuple-element.116) | copy-start | bytes 122884
  101.9 1.4 %copy-start.26 = (f32[1,16,5,128]{3,2,1,0:T(8,128)S(1)}, f32[1,16,5,128]{3,2,1,0:T(8,128)}, u32[]{:S(2)}) copy-start(f32[1,16,5,128]{3,2,1,0:T(8,128)} %get-tuple-element.117) | copy-start | bytes 122884
  101.9 1.4 %copy-start.31 = (f32[1,16,4,128]{3,2,1,0:T(4,128)S(1)}, f32[1,16,4,128]{3,2,1,0:T(4,128)}, u32[]{:S(2)}) copy-start(f32[1,16,4,128]{3,2,1,0:T(4,128)} %get-tuple-element.120) | copy-start | bytes 98308
  101.9 1.4 %copy-start.32 = (f32[1,16,4,128]{3,2,1,0:T(4,128)S(1)}, f32[1,16,4,128]{3,2,1,0:T(4,128)}, u32[]{:S(2)}) copy-start(f32[1,16,4,128]{3,2,1,0:T(4,128)} %get-tuple-element.121) | copy-start | bytes 98308
  101.9 1.4 copy-start.33
  101.9 1.4 copy-start.34
  102.0 1.4 copy-start.45
  102.0 1.4 copy-start.46
  102.0 1.4 copy-start.57
  102.0 1.5 %copy-start.60 = (f32[16,32,128]{2,1,0:T(8,128)S(1)}, f32[16,32,128]{2,1,0:T(8,128)}, u32[]{:S(2)}) copy-start(f32[16,32,128]{2,1,0:T(8,128)} %param.12) | copy-start | bytes 786436
  102.0 1.6 %copy-start.63 = (f32[1,16,32,128]{3,2,1,0:T(8,128)S(1)}, f32[1,16,32,128]{3,2,1,0:T(8,128)}, u32[]{:S(2)}) copy-start(f32[1,16,32,128]{3,2,1,0:T(8,128)} %get-tuple-element.166) | copy-start | bytes 786436
  110.1 1.9 %copy-start.41 = (f32[10,10]{0,1:T(8,128)S(1)}, f32[10,10]{0,1:T(8,128)}, u32[]{:S(2)}) copy-start(f32[10,10]{0,1:T(8,128)} %fusion.344) | copy-start | bytes 1204
  111.9 1.5 %copy-start.54 = (bf16[10,10]{1,0:T(8,128)(2,1)S(1)}, bf16[10,10]{1,0:T(8,128)(2,1)}, u32[]{:S(2)}) copy-start(bf16[10,10]{1,0:T(8,128)(2,1)} %copy.43) | copy-start | bytes 604
  113.4 10.2 %copy-start.51 = (pred[32]{0:T(512)(128)(4,1)S(1)}, pred[32]{0:T(512)(128)(4,1)}, u32[]{:S(2)}) copy-start(pred[32]{0:T(512)(128)(4,1)} %copy-done.50) | copy-start | bytes 100
  113.8 9.8 %copy-start.49 = (pred[32]{0:T(512)(128)(4,1)S(1)}, pred[32]{0:T(512)(128)(4,1)}, u32[]{:S(2)}) copy-start(pred[32]{0:T(512)(128)(4,1)} %copy-done.48) | copy-start | bytes 100
  113.8 8.3 %collective-permute-start.6 = (f32[1,6,32,128]{3,2,1,0:T(8,128)S(1)}, f32[1,6,32,128]{3,2,1,0:T(8,128)S(1)}, u32[]{:S(2)}, u32[]{:S(2)}) collective-permute-start(f32[1,6,32,128]{3,2,1,0:T(8,128)S(1)} %get-tuple-element.111), channel_id=1, source_target_pairs={{0,16},{16,32},{32,48},{48,64},{64,80},{80,96},{96,112},{112,128},... | collective-permute-start | bytes 294920 | tf_op jit(solution)/shard_map/ppermute | solution.py:21
  113.9 9.0 %collective-permute-start.5 = (f32[1,6,32,128]{3,2,1,0:T(8,128)S(1)}, f32[1,6,32,128]{3,2,1,0:T(8,128)S(1)}, u32[]{:S(2)}, u32[]{:S(2)}) collective-permute-start(f32[1,6,32,128]{3,2,1,0:T(8,128)S(1)} %get-tuple-element.110), channel_id=1, source_target_pairs={{16,0},{32,16},{48,32},{64,48},{80,64},{96,80},{112,96},{128,112},... | collective-permute-start | bytes 294920 | tf_op jit(solution)/shard_map/ppermute | solution.py:22
  124.5 1.1 copy-start.4
  124.5 1.2 copy-start.5
  124.5 1.2 copy-start.6
  124.5 1.3 copy-start.7
  124.5 1.4 %copy-start.8 = (f32[1,16,26,128]{3,2,1,0:T(8,128)S(1)}, f32[1,16,26,128]{3,2,1,0:T(8,128)}, u32[]{:S(2)}) copy-start(f32[1,16,26,128]{3,2,1,0:T(8,128)} %get-tuple-element.89) | copy-start | bytes 638980
  124.5 1.4 %copy-start.19 = (f32[1,16,5,128]{3,2,1,0:T(8,128)S(1)}, f32[1,16,5,128]{3,2,1,0:T(8,128)}, u32[]{:S(2)}) copy-start(f32[1,16,5,128]{3,2,1,0:T(8,128)} %get-tuple-element.90) | copy-start | bytes 122884
  124.5 1.4 %copy-start.20 = (f32[1,16,5,128]{3,2,1,0:T(8,128)S(1)}, f32[1,16,5,128]{3,2,1,0:T(8,128)}, u32[]{:S(2)}) copy-start(f32[1,16,5,128]{3,2,1,0:T(8,128)} %get-tuple-element.91) | copy-start | bytes 122884
  124.5 1.4 copy-start.21
  124.5 1.4 %copy-start.22 = (f32[1,16,6,128]{3,2,1,0:T(8,128)S(1)}, f32[1,16,6,128]{3,2,1,0:T(8,128)}, u32[]{:S(2)}) copy-start(f32[1,16,6,128]{3,2,1,0:T(8,128)} %get-tuple-element.87) | copy-start | bytes 147460
  124.5 1.4 copy-start.28
  124.6 1.3 copy-start.29
  124.6 1.3 copy-start.30
  124.6 1.3 copy-start.36
  124.6 1.3 copy-start.37
  124.6 1.3 copy-start.44
  124.6 1.3 copy-start.58
  124.6 1.5 %copy-start.61 = (f32[16,32,128]{2,1,0:T(8,128)S(1)}, f32[16,32,128]{2,1,0:T(8,128)}, u32[]{:S(2)}) copy-start(f32[16,32,128]{2,1,0:T(8,128)} %param.12) | copy-start | bytes 786436
  124.6 1.6 %copy-start.64 = (f32[1,16,32,128]{3,2,1,0:T(8,128)S(1)}, f32[1,16,32,128]{3,2,1,0:T(8,128)}, u32[]{:S(2)}) copy-start(f32[1,16,32,128]{3,2,1,0:T(8,128)} %get-tuple-element.166) | copy-start | bytes 786436
  (9 other events, 8.5 us)
Sparse Core Ops, SparseCore 0:
  30.9 35.8 all-gather.2
where the time goes:
time: 136 us
  waiting for transfers between devices  38.2 us (28%)
  local copies, waits for them, and re-layouts  36.5 us (27%)
  starting transfers between devices  22.7 us (17%)
  matrix products  14.8 us (11%)
  between operations  14.7 us (11%)
  other arithmetic  8.83 us (6%)
    all_gather x1, waiting for transfers between devices, shards(): gathered = lax.all_gather(packed[0], 'states', axis=0, tiled=True)  30 us
    slice x36, local copies, waits for them, and re-layouts, laplacian(): jnp.roll(interior, k, 2)  21.6 us
    ppermute x3, starting transfers between devices, padded_2(): after = lax.ppermute(initial, axis, down)  17.5 us
    dot_general x3, matrix products, nonlocal_part(): lax.dot_general(selector, projected, (((0,), (0,)), ((), ())), preferred_...  8.52 us
    ppermute x3, waiting for transfers between devices, padded_2(): before = lax.ppermute(last, axis, up)  7.08 us
    ppermute x1, starting transfers between devices, shards(): packed = lax.ppermute(packed, ('grid', 'states'), pairs)  5.15 us
    dot_general x3, matrix products, nonlocal_part(): lax.dot_general(proj_rows, picked, (((1,), (1,)), ((), ())), preferred_el...  4.03 us
    unnamed x131, local copies, waits for them, and re-layouts  3.33 us
  transfers between devices with their start and end apart: 8, of which 4 were waited for; matrix products, arithmetic and copies ran while one was open for 14% of the time, Pallas kernels for 0%

commit v1 on v0

--- a/solution.py
+++ b/solution.py
@@ -9,6 +9,13 @@
 MIXED_WEIGHT = 0.7
 CENTER = 12.0
 HALF_WIDTH = 8.0
+
+
+def exchange_gather(block, axis, d):
+    size = lax.axis_size(axis)
+    shards = jnp.stack([block for _ in range(size)])
+    shards = lax.all_to_all(shards, axis, split_axis=0, concat_axis=0)
+    return jnp.concatenate(shards, axis=d)
 
 
 def padded_2(shard, sides, width):
@@ -102,7 +109,7 @@
     packed = jnp.concatenate([projectors, gain_lanes], axis=3)
     pairs = [(o * n_states + t, t * n_states + o) for o in range(n_grid) for t in range(n_states)]
     packed = lax.ppermute(packed, ("grid", "states"), pairs)
-    gathered = lax.all_gather(packed[0], "states", axis=0, tiled=True)
+    gathered = exchange_gather(packed[0], "states", 0)
     gathered = gathered.reshape(n_states * slot_pairs, proj_count, line_span + 128)
     atom_pack = jnp.take(gathered, atom_slot, axis=0)
     proj_rows = atom_pack[:, :, :line_span].reshape(home_count * proj_count, line_span)

time: 136 us -> 129 us (0.949)
  between operations: 14.7 us -> 1.42 us
  starting transfers between devices: 22.7 us -> 29.4 us
  waiting for transfers between devices: 38.2 us -> 34.3 us
  local copies, waits for them, and re-layouts: 36.5 us -> 40 us
    all_gather x1 -> x0, waiting for transfers between devices: 30 us -> none  [shards(): gathered = lax.all_gather(packed[0], 'states', axis=0, tiled=True)]
    all_to_all x0 -> x1, waiting for transfers between devices: none -> 26.6 us  [exchange_gather(): shards = lax.all_to_all(shards, axis, split_axis=0, concat_axis=0)]
    all_to_all x0 -> x1, starting transfers between devices: none -> 6.57 us  [exchange_gather(): shards = lax.all_to_all(shards, axis, split_axis=0, concat_axis=0)]
    gather x1, local copies, waits for them, and re-layouts: 2.24 us -> 0.63 us  [shards(): atom_pack = jnp.take(gathered, atom_slot, axis=0)]
    another operation x0 -> x1, local copies, waits for them, and re-layouts: none -> 1.49 us  [exchange_gather(): shards = jnp.stack([block for _ in range(size)])]
    unnamed x131 -> x149, local copies, waits for them, and re-layouts: 3.33 us -> 4.12 us
  transfers between devices with their start and end apart: 8 -> 8, of which waited for: 4 -> 4; matrix products, arithmetic and copies ran while one was open for 14% -> 17% of each run, Pallas kernels for 0% -> 0%
where the time goes in v1:
time: 129 us; the launch traced here: 128 us
  local copies, waits for them, and re-layouts  40 us (31%)
  waiting for transfers between devices  34.3 us (27%)
  starting transfers between devices  29.4 us (23%)
  matrix products  14.7 us (11%)
  other arithmetic  8.26 us (6%)
  between operations  1.42 us (1%)
    all_to_all x1, waiting for transfers between devices, exchange_gather(): shards = lax.all_to_all(shards, axis, split_axis=0, concat_axis=0)  26.6 us
    slice x36, local copies, waits for them, and re-layouts, laplacian(): jnp.roll(interior, k, 2)  22.5 us
    ppermute x3, starting transfers between devices, padded_2(): after = lax.ppermute(initial, axis, down)  17.6 us
    dot_general x3, matrix products, nonlocal_part(): lax.dot_general(selector, projected, (((0,), (0,)), ((), ())), preferred_...  8.45 us
    ppermute x3, waiting for transfers between devices, padded_2(): before = lax.ppermute(last, axis, up)  6.86 us
    all_to_all x1, starting transfers between devices, exchange_gather(): shards = lax.all_to_all(shards, axis, split_axis=0, concat_axis=0)  6.57 us
    ppermute x1, starting transfers between devices, shards(): packed = lax.ppermute(packed, ('grid', 'states'), pairs)  5.15 us
    unnamed x149, local copies, waits for them, and re-layouts  4.12 us
  transfers between devices with their start and end apart: 8, of which 4 were waited for; matrix products, arithmetic and copies ran while one was open for 17% of the time, Pallas kernels for 0%

profile of v1, /device:TPU:2, one launch (start us, length us, event | category | flops | bytes accessed | tf_op | source)
XLA Modules:
  0.0 128.1 jit_solution(15352531437705321686)
XLA Ops:
  0.0 0.8 copy.71
  0.8 0.9 fusion.328
  1.7 5.2 %collective-permute-start.2 = (bf16[1,2,8,4224]{3,2,1,0:T(8,128)(2,1)S(1)}, bf16[1,2,8,4224]{3,2,1,0:T(8,128)(2,1)S(1)}, u32[]{:S(2)}, u32[]{:S(2)}) collective-permute-start(bf16[1,2,8,4224]{3,2,1,0:T(8,128)(2,1)S(1)} %fusion.328), channel_id=1, source_target_pairs={{0,0},{1,16},{2,32},{3,48},{4,64},{5,80},{6,96},{7,112},{8,128},{9... | collective-permute-start | bytes 405512 | tf_op jit(solution)/shard_map/ppermute | solution.py:111
  6.9 1.0 fusion.419
  7.8 6.3 %collective-permute-start = (f32[1,6,32,128]{3,2,1,0:T(8,128)S(1)}, f32[1,6,32,128]{3,2,1,0:T(8,128)S(1)}, u32[]{:S(2)}, u32[]{:S(2)}) collective-permute-start(f32[1,6,32,128]{3,2,1,0:T(8,128)S(1)} %get-tuple-element.164), channel_id=1, source_target_pairs={{16,0},{32,16},{48,32},{64,48},{80,64},{96,80},{112,96},{128,112},... | collective-permute-start | bytes 294920 | tf_op jit(solution)/shard_map/ppermute | solution.py:29
  14.1 1.0 convert_element_type.119
  15.4 0.8 fusion.408
  16.2 0.7 fusion.407
  16.9 0.8 fusion.410
  17.7 0.7 fusion.409
  18.4 0.8 fusion.412
  19.2 0.7 fusion.411
  19.9 0.9 fusion.414
  20.8 0.6 fusion.413
  21.4 0.8 fusion.416
  22.2 0.6 fusion.415
  22.9 0.9 fusion.418
  25.5 0.7 reshape.2364
  26.2 0.7 copy.51
  28.5 0.6 fusion.374
  29.2 1.5 %stack.3 = bf16[16,2,8,4224]{3,2,1,0:T(8,128)(2,1)} broadcast(bf16[2,8,4224]{2,1,0:T(8,128)(2,1)S(1)} %bitcast.112), dimensions={1,2,3} | broadcast | bytes 2297856 | tf_op jit(solution)/shard_map/stack | solution.py:16
  30.7 6.6 %all-to-all-start = ((bf16[16,2,8,4224]{3,2,1,0:T(8,128)(2,1)}), bf16[16,2,8,4224]{3,2,1,0:T(8,128)(2,1)S(1)}, u32[]{:S(2)}, u32[]{:S(2)}) async-start(bf16[16,2,8,4224]{3,2,1,0:T(8,128)(2,1)} %stack.3), calls=%async_computation | async-start | bytes 4325376 | tf_op jit(solution)/shard_map/all_to_all | solution.py:17
  37.8 0.7 copy-done.18
  38.6 1.6 %fusion.76 = f32[1,28,32,128]{3,2,1,0:T(8,128)} fusion(f32[1,6,32,128]{3,2,1,0:T(8,128)S(1)} %fusion.334, f32[1,16,32,128]{3,2,1,0:T(8,128)S(1)} %copy-done, f32[1,6,32,128]{3,2,1,0:T(8,128)S(1)} %fusion.333, f32[1,28,31,128]{3,2,1,0:T(8,128)S(1)} %get-tuple-element.85, f32[1,28,31,128]{3,2,1,0:T(8,128)S(1)} %get-tuple-element.84, ...), kind=kLoop, calls=%fused_computation.173 | loop fusion | flops 3784704 | bytes 6393856 | tf_op jit(solution)/shard_map/add | solution.py:75
  40.2 26.6 %all-to-all-done = bf16[16,2,8,4224]{3,2,1,0:T(8,128)(2,1)S(1)} async-done(((bf16[16,2,8,4224]{3,2,1,0:T(8,128)(2,1)}), bf16[16,2,8,4224]{3,2,1,0:T(8,128)(2,1)S(1)}, u32[]{:S(2)}, u32[]{:S(2)}) %all-to-all-start) | async-done | bytes 2162720 | tf_op jit(solution)/shard_map/all_to_all | solution.py:17
  66.7 0.6 gather_fusion
  68.3 1.3 %fusion.48 = f32[10,8]{0,1:T(8,128)S(1)} fusion(bf16[10,4096,1]{1,0,2:T(8,128)(2,1)S(1)} %copy-done.19, bf16[10,8,4224]{2,0,1:T(8,128)(2,1)S(1)} %copy_select_fusion, f32[10,10]{0,1:T(8,128)S(1)} %fusion.344), kind=kOutput, calls=%fused_computation.74 | convolution fusion | flops 6555120 | bytes 1188160 | tf_op jit(solution)/shard_map/dot_general | solution.py:136
  70.9 4.3 %broadcast_multiply_fusion = (f32[1,16,32,128]{3,2,1,0:T(8,128)S(1)}, bf16[1,16,32,128]{3,2,1,0:T(8,128)(2,1)S(1)}, f32[1,16,32,128]{3,2,1,0:T(8,128)}) fusion(f32[1,16,32,128]{3,2,1,0:T(8,128)S(1)} %copy-done, bf16[320,128,1]{1,0,2:T(8,128)(2,1)S(1)} %reshape.2366, s32[16,32]{1,0:T(8,128)S(1)} %multiply_add_fusion, s32[320]{0:T(512)S(1)} %copy-done.64, ...), kind=kOutput, calls=%fused_computation.493 | convolution fusion | flops 49053696 | bytes 7752960 | tf_op jit(solution)/shard_map/dot_general | solution.py:146
  75.2 0.7 fusion.406
  75.9 0.7 fusion.394
  76.6 0.7 fusion.396
  77.2 0.7 fusion.399
  78.0 0.6 fusion.398
  78.6 0.8 fusion.401
  79.4 0.6 fusion.400
  80.0 0.8 fusion.403
  80.9 0.6 fusion.402
  81.5 0.8 fusion.405
  82.7 1.3 %fusion.49 = f32[10,8]{0,1:T(8,128)S(1)} fusion(bf16[10,4096,1]{1,0,2:T(8,128)(2,1)S(1)} %reshape.2367, bf16[10,8,4224]{2,0,1:T(8,128)(2,1)S(1)} %copy_select_fusion, f32[10,10]{0,1:T(8,128)S(1)} %copy-done.47), kind=kOutput, calls=%fused_computation.75 | convolution fusion | flops 6555120 | bytes 1188160 | tf_op jit(solution)/shard_map/dot_general | solution.py:136
  84.6 5.6 %collective-permute-start.3 = (f32[1,6,32,128]{3,2,1,0:T(8,128)S(1)}, f32[1,6,32,128]{3,2,1,0:T(8,128)S(1)}, u32[]{:S(2)}, u32[]{:S(2)}) collective-permute-start(f32[1,6,32,128]{3,2,1,0:T(8,128)S(1)} %get-tuple-element.136), channel_id=1, source_target_pairs={{16,0},{32,16},{48,32},{64,48},{80,64},{96,80},{112,96},{128,112},... | collective-permute-start | bytes 294920 | tf_op jit(solution)/shard_map/ppermute | solution.py:29
  90.2 0.6 fusion.404
  90.8 0.7 reshape.2369
  91.5 0.9 collective-permute-done.3
  93.1 5.6 %collective-permute-done.4 = f32[1,6,32,128]{3,2,1,0:T(8,128)S(1)} collective-permute-done((f32[1,6,32,128]{3,2,1,0:T(8,128)}, f32[1,6,32,128]{3,2,1,0:T(8,128)S(1)}, u32[]{:S(2)}, u32[]{:S(2)}) %collective-permute-start.4) | collective-permute-done | bytes 98336 | tf_op jit(solution)/shard_map/ppermute | solution.py:28
  98.7 0.7 gather_fusion.4
  99.4 0.7 fusion.332
  100.2 0.7 fusion.331
  101.9 0.8 fusion.67
  103.4 1.4 %fusion.420 = (bf16[1,16,32,128]{3,2,1,0:T(8,128)(2,1)S(1)}, f32[1,16,32,128]{3,2,1,0:T(8,128)S(1)}) fusion(f32[1,16,32,128]{3,2,1,0:T(8,128)S(1)} %copy-done, f32[1,16,32,128]{3,2,1,0:T(8,128)S(1)} %copy-done.72, bf16[320,128,1]{1,0,2:T(8,128)(2,1)S(1)} %copy-done.21, s32[16,32]{1,0:T(8,128)S(1)} %multiply_add_fusion, s32[320]{0:T(512)S(1)} %copy-done.66, ...), kind=kOutput, calls=%fused_computation.611 | convolution fusion | flops 49119232 | bytes 8015104 | tf_op jit(solution)/shard_map/dot_general | solution.py:146
  104.9 0.6 fusion.389
  105.6 0.6 fusion.387
  106.2 0.6 fusion.385
  106.9 0.8 fusion.386
  107.7 0.7 fusion.383
  108.4 0.8 fusion.384
  109.2 0.7 fusion.381
  109.9 0.8 fusion.382
  111.1 1.3 %fusion.50 = f32[10,8]{0,1:T(8,128)S(1)} fusion(bf16[10,4096,1]{1,0,2:T(8,128)(2,1)S(1)} %reshape.2370, bf16[10,8,4224]{2,0,1:T(8,128)(2,1)S(1)} %copy_select_fusion, f32[10,10]{0,1:T(8,128)S(1)} %copy-done.48), kind=kOutput, calls=%fused_computation.76 | convolution fusion | flops 6555120 | bytes 1188160 | tf_op jit(solution)/shard_map/dot_general | solution.py:136
  113.0 5.6 %collective-permute-start.5 = (f32[1,6,32,128]{3,2,1,0:T(8,128)S(1)}, f32[1,6,32,128]{3,2,1,0:T(8,128)S(1)}, u32[]{:S(2)}, u32[]{:S(2)}) collective-permute-start(f32[1,6,32,128]{3,2,1,0:T(8,128)S(1)} %get-tuple-element.110), channel_id=1, source_target_pairs={{16,0},{32,16},{48,32},{64,48},{80,64},{96,80},{112,96},{128,112},... | collective-permute-start | bytes 294920 | tf_op jit(solution)/shard_map/ppermute | solution.py:29
  119.2 0.7 reshape.2372
  119.9 1.3 %collective-permute-done.6 = f32[1,6,32,128]{3,2,1,0:T(8,128)S(1)} collective-permute-done((f32[1,6,32,128]{3,2,1,0:T(8,128)S(1)}, f32[1,6,32,128]{3,2,1,0:T(8,128)S(1)}, u32[]{:S(2)}, u32[]{:S(2)}) %collective-permute-start.6) | collective-permute-done | bytes 98336 | tf_op jit(solution)/shard_map/ppermute | solution.py:28
  121.3 0.7 gather_fusion.6
  123.8 0.8 fusion.58
  125.3 2.8 %fusion.27 = f32[1,16,32,128]{3,2,1,0:T(8,128)} fusion(bf16[320,128,1]{1,0,2:T(8,128)(2,1)S(1)} %copy-done.20, s32[16,32]{1,0:T(8,128)S(1)} %multiply_add_fusion, s32[320]{0:T(512)S(1)} %copy-done.67, f32[1,16,32,128]{3,2,1,0:T(8,128)S(1)} %get-tuple-element.168, f32[1,6,32,128]{3,2,1,0:T(8,128)S(1)} %fusion.329, f32[1,6,32,128]{3,2,1,0:T(8,128)S(1)} %fusion.330, ...), kind=kOutput, calls=%fused_computation.61 | convolution fusion | flops 49119232 | bytes 7621888 | tf_op jit(solution)/shard_map/dot_general | solution.py:146
  (240 shorter events, 12.7 us)
Async XLA Ops:
  0.0 15.4 %copy-start = (f32[1,16,32,128]{3,2,1,0:T(8,128)S(1)}, f32[1,16,32,128]{3,2,1,0:T(8,128)}, u32[]{:S(2)}) copy-start(f32[1,16,32,128]{3,2,1,0:T(8,128)} %param.11) | copy-start | bytes 786436
  0.0 15.2 %copy-start.71 = (s32[32]{0:T(128)S(1)}, s32[32]{0:T(128)}, u32[]{:S(2)}) copy-start(s32[32]{0:T(128)} %param.17) | copy-start | bytes 388
  1.7 27.5 %collective-permute-start.2 = (bf16[1,2,8,4224]{3,2,1,0:T(8,128)(2,1)S(1)}, bf16[1,2,8,4224]{3,2,1,0:T(8,128)(2,1)S(1)}, u32[]{:S(2)}, u32[]{:S(2)}) collective-permute-start(bf16[1,2,8,4224]{3,2,1,0:T(8,128)(2,1)S(1)} %fusion.328), channel_id=1, source_target_pairs={{0,0},{1,16},{2,32},{3,48},{4,64},{5,80},{6,96},{7,112},{8,128},{9... | collective-permute-start | bytes 405512 | tf_op jit(solution)/shard_map/ppermute | solution.py:111
  7.8 19.1 %collective-permute-start = (f32[1,6,32,128]{3,2,1,0:T(8,128)S(1)}, f32[1,6,32,128]{3,2,1,0:T(8,128)S(1)}, u32[]{:S(2)}, u32[]{:S(2)}) collective-permute-start(f32[1,6,32,128]{3,2,1,0:T(8,128)S(1)} %get-tuple-element.164), channel_id=1, source_target_pairs={{16,0},{32,16},{48,32},{64,48},{80,64},{96,80},{112,96},{128,112},... | collective-permute-start | bytes 294920 | tf_op jit(solution)/shard_map/ppermute | solution.py:29
  14.1 12.9 %collective-permute-start.1 = (f32[1,6,32,128]{3,2,1,0:T(8,128)S(1)}, f32[1,6,32,128]{3,2,1,0:T(8,128)S(1)}, u32[]{:S(2)}, u32[]{:S(2)}) collective-permute-start(f32[1,6,32,128]{3,2,1,0:T(8,128)S(1)} %get-tuple-element.165), channel_id=1, source_target_pairs={{0,16},{16,32},{32,48},{48,64},{64,80},{80,96},{96,112},{112,128},... | collective-permute-start | bytes 294920 | tf_op jit(solution)/shard_map/ppermute | solution.py:28
  15.1 52.6 %copy-start.46 = (f32[10,10]{0,1:T(8,128)}, f32[10,10]{0,1:T(8,128)S(1)}, u32[]{:S(2)}) copy-start(f32[10,10]{0,1:T(8,128)S(1)} %fusion.344) | copy-start | bytes 1204
  15.3 13.0 %copy-start.55 = (pred[32]{0:T(512)(128)(4,1)}, pred[32]{0:T(512)(128)(4,1)S(1)}, u32[]{:S(2)}) copy-start(pred[32]{0:T(512)(128)(4,1)S(1)} %compare_and_fusion.1) | copy-start | bytes 100
  15.4 13.0 %copy-start.57 = (pred[32]{0:T(512)(128)(4,1)}, pred[32]{0:T(512)(128)(4,1)S(1)}, u32[]{:S(2)}) copy-start(pred[32]{0:T(512)(128)(4,1)S(1)} %compare_and_fusion) | copy-start | bytes 100
  21.4 3.0 %copy-start.68 = (s32[10]{0:T(128)S(1)}, s32[10]{0:T(128)}, u32[]{:S(2)}) copy-start(s32[10]{0:T(128)} %param.15) | copy-start | bytes 124
  21.4 3.7 %copy-start.45 = (s32[10,32]{1,0:T(8,128)S(1)}, s32[10,32]{1,0:T(8,128)}, u32[]{:S(2)}) copy-start(s32[10,32]{1,0:T(8,128)} %param.16) | copy-start | bytes 3844
  25.2 1.7 %copy-start.63 = (s32[320]{0:T(512)}, s32[320]{0:T(512)S(1)}, u32[]{:S(2)}) copy-start(s32[320]{0:T(512)S(1)} %eq.101) | copy-start | bytes 3844
  26.9 1.6 %copy-start.54 = (s32[1024]{0:T(1024)}, s32[1024]{0:T(1024)S(1)}, u32[]{:S(2)}) copy-start(s32[1024]{0:T(1024)S(1)} %pad_clamp_fusion.1) | copy-start | bytes 12292
  30.7 36.0 %all-to-all-start = ((bf16[16,2,8,4224]{3,2,1,0:T(8,128)(2,1)}), bf16[16,2,8,4224]{3,2,1,0:T(8,128)(2,1)S(1)}, u32[]{:S(2)}, u32[]{:S(2)}) async-start(bf16[16,2,8,4224]{3,2,1,0:T(8,128)(2,1)} %stack.3), calls=%async_computation | async-start | bytes 4325376 | tf_op jit(solution)/shard_map/all_to_all | solution.py:17
  40.2 27.2 %copy-start.62 = (pred[10]{0:T(512)(128)(4,1)S(1)}, pred[10]{0:T(512)(128)(4,1)}, u32[]{:S(2)}) copy-start(pred[10]{0:T(512)(128)(4,1)} %get-tuple-element.18) | copy-start | bytes 34
  67.6 2.1 %copy-start.59 = (bf16[10,10]{1,0:T(8,128)(2,1)S(1)}, bf16[10,10]{1,0:T(8,128)(2,1)}, u32[]{:S(2)}) copy-start(bf16[10,10]{1,0:T(8,128)(2,1)} %copy.51) | copy-start | bytes 604
  69.6 1.2 copy-start.4
  69.6 1.2 copy-start.22
  69.6 1.2 copy-start.23
  80.0 2.3 %copy-start.65 = (s32[320]{0:T(512)S(1)}, s32[320]{0:T(512)}, u32[]{:S(2)}) copy-start(s32[320]{0:T(512)} %copy-done.63) | copy-start | bytes 3844
  80.9 1.8 %copy-start.47 = (f32[10,10]{0,1:T(8,128)S(1)}, f32[10,10]{0,1:T(8,128)}, u32[]{:S(2)}) copy-start(f32[10,10]{0,1:T(8,128)} %copy-done.46) | copy-start | bytes 1204
  82.7 1.4 %copy-start.60 = (bf16[10,10]{1,0:T(8,128)(2,1)S(1)}, bf16[10,10]{1,0:T(8,128)(2,1)}, u32[]{:S(2)}) copy-start(bf16[10,10]{1,0:T(8,128)(2,1)} %copy.51) | copy-start | bytes 604
  84.6 7.9 %collective-permute-start.3 = (f32[1,6,32,128]{3,2,1,0:T(8,128)S(1)}, f32[1,6,32,128]{3,2,1,0:T(8,128)S(1)}, u32[]{:S(2)}, u32[]{:S(2)}) collective-permute-start(f32[1,6,32,128]{3,2,1,0:T(8,128)S(1)} %get-tuple-element.136), channel_id=1, source_target_pairs={{16,0},{32,16},{48,32},{64,48},{80,64},{96,80},{112,96},{128,112},... | collective-permute-start | bytes 294920 | tf_op jit(solution)/shard_map/ppermute | solution.py:29
  90.2 8.4 %collective-permute-start.4 = (f32[1,6,32,128]{3,2,1,0:T(8,128)}, f32[1,6,32,128]{3,2,1,0:T(8,128)S(1)}, u32[]{:S(2)}, u32[]{:S(2)}) collective-permute-start(f32[1,6,32,128]{3,2,1,0:T(8,128)} %get-tuple-element.137), channel_id=1, source_target_pairs={{0,16},{16,32},{32,48},{48,64},{64,80},{80,96},{96,112},{112,128},... | collective-permute-start | bytes 294920 | tf_op jit(solution)/shard_map/ppermute | solution.py:28
  101.7 1.2 copy-start.15
  101.7 1.3 %copy-start.16 = (f32[1,16,31,128]{3,2,1,0:T(8,128)S(1)}, f32[1,16,31,128]{3,2,1,0:T(8,128)}, u32[]{:S(2)}) copy-start(f32[1,16,31,128]{3,2,1,0:T(8,128)} %get-tuple-element.134) | copy-start | bytes 761860
  101.7 1.4 %copy-start.17 = (f32[1,16,31,128]{3,2,1,0:T(8,128)S(1)}, f32[1,16,31,128]{3,2,1,0:T(8,128)}, u32[]{:S(2)}) copy-start(f32[1,16,31,128]{3,2,1,0:T(8,128)} %get-tuple-element.135) | copy-start | bytes 761860
  101.7 1.4 %copy-start.21 = (bf16[320,128,1]{1,0,2:T(8,128)(2,1)S(1)}, bf16[320,128,1]{1,0,2:T(8,128)(2,1)}, u32[]{:S(2)}) copy-start(bf16[320,128,1]{1,0,2:T(8,128)(2,1)} %reshape.2369) | copy-start | bytes 245764
  101.7 1.4 %copy-start.29 = (f32[1,16,6,128]{3,2,1,0:T(8,128)S(1)}, f32[1,16,6,128]{3,2,1,0:T(8,128)}, u32[]{:S(2)}) copy-start(f32[1,16,6,128]{3,2,1,0:T(8,128)} %get-tuple-element.112) | copy-start | bytes 147460
  101.7 1.4 %copy-start.30 = (f32[1,16,6,128]{3,2,1,0:T(8,128)S(1)}, f32[1,16,6,128]{3,2,1,0:T(8,128)}, u32[]{:S(2)}) copy-start(f32[1,16,6,128]{3,2,1,0:T(8,128)} %get-tuple-element.113) | copy-start | bytes 147460
  101.7 1.4 %copy-start.31 = (f32[1,16,5,128]{3,2,1,0:T(8,128)S(1)}, f32[1,16,5,128]{3,2,1,0:T(8,128)}, u32[]{:S(2)}) copy-start(f32[1,16,5,128]{3,2,1,0:T(8,128)} %get-tuple-element.116) | copy-start | bytes 122884
  101.7 1.4 %copy-start.32 = (f32[1,16,5,128]{3,2,1,0:T(8,128)S(1)}, f32[1,16,5,128]{3,2,1,0:T(8,128)}, u32[]{:S(2)}) copy-start(f32[1,16,5,128]{3,2,1,0:T(8,128)} %get-tuple-element.117) | copy-start | bytes 122884
  101.8 1.4 %copy-start.38 = (f32[1,16,4,128]{3,2,1,0:T(4,128)S(1)}, f32[1,16,4,128]{3,2,1,0:T(4,128)}, u32[]{:S(2)}) copy-start(f32[1,16,4,128]{3,2,1,0:T(4,128)} %get-tuple-element.121) | copy-start | bytes 98308
  101.8 1.4 %copy-start.39 = (f32[1,16,3,128]{3,2,1,0:T(4,128)S(1)}, f32[1,16,3,128]{3,2,1,0:T(4,128)}, u32[]{:S(2)}) copy-start(f32[1,16,3,128]{3,2,1,0:T(4,128)} %get-tuple-element.124) | copy-start | bytes 73732
  101.8 1.4 %copy-start.40 = (f32[1,16,3,128]{3,2,1,0:T(4,128)S(1)}, f32[1,16,3,128]{3,2,1,0:T(4,128)}, u32[]{:S(2)}) copy-start(f32[1,16,3,128]{3,2,1,0:T(4,128)} %get-tuple-element.125) | copy-start | bytes 73732
  101.8 1.4 %copy-start.43 = (f32[1,16,2,128]{3,2,1,0:T(2,128)S(1)}, f32[1,16,2,128]{3,2,1,0:T(2,128)}, u32[]{:S(2)}) copy-start(f32[1,16,2,128]{3,2,1,0:T(2,128)} %get-tuple-element.128) | copy-start | bytes 49156
  101.8 1.4 %copy-start.44 = (f32[1,16,2,128]{3,2,1,0:T(2,128)S(1)}, f32[1,16,2,128]{3,2,1,0:T(2,128)}, u32[]{:S(2)}) copy-start(f32[1,16,2,128]{3,2,1,0:T(2,128)} %get-tuple-element.129) | copy-start | bytes 49156
  101.8 1.4 %copy-start.52 = (f32[1,16,1,128]{3,2,1,0:T(1,128)S(1)}, f32[1,16,1,128]{3,2,1,0:T(1,128)}, u32[]{:S(2)}) copy-start(f32[1,16,1,128]{3,2,1,0:T(1,128)} %get-tuple-element.132) | copy-start | bytes 24580
  101.8 1.4 %copy-start.53 = (f32[1,16,1,128]{3,2,1,0:T(1,128)S(1)}, f32[1,16,1,128]{3,2,1,0:T(1,128)}, u32[]{:S(2)}) copy-start(f32[1,16,1,128]{3,2,1,0:T(1,128)} %get-tuple-element.133) | copy-start | bytes 24580
  101.8 1.4 %copy-start.66 = (s32[320]{0:T(512)S(1)}, s32[320]{0:T(512)}, u32[]{:S(2)}) copy-start(s32[320]{0:T(512)} %copy-done.63) | copy-start | bytes 3844
  101.8 1.5 %copy-start.69 = (f32[16,32,128]{2,1,0:T(8,128)S(1)}, f32[16,32,128]{2,1,0:T(8,128)}, u32[]{:S(2)}) copy-start(f32[16,32,128]{2,1,0:T(8,128)} %param.12) | copy-start | bytes 786436
  101.8 1.6 %copy-start.72 = (f32[1,16,32,128]{3,2,1,0:T(8,128)S(1)}, f32[1,16,32,128]{3,2,1,0:T(8,128)}, u32[]{:S(2)}) copy-start(f32[1,16,32,128]{3,2,1,0:T(8,128)} %get-tuple-element.166) | copy-start | bytes 786436
  109.2 1.9 %copy-start.48 = (f32[10,10]{0,1:T(8,128)S(1)}, f32[10,10]{0,1:T(8,128)}, u32[]{:S(2)}) copy-start(f32[10,10]{0,1:T(8,128)} %copy-done.46) | copy-start | bytes 1204
  111.0 1.4 %copy-start.61 = (bf16[10,10]{1,0:T(8,128)(2,1)S(1)}, bf16[10,10]{1,0:T(8,128)(2,1)}, u32[]{:S(2)}) copy-start(bf16[10,10]{1,0:T(8,128)(2,1)} %copy.51) | copy-start | bytes 604
  112.9 9.8 %copy-start.58 = (pred[32]{0:T(512)(128)(4,1)S(1)}, pred[32]{0:T(512)(128)(4,1)}, u32[]{:S(2)}) copy-start(pred[32]{0:T(512)(128)(4,1)} %copy-done.57) | copy-start | bytes 100
  112.9 9.8 %copy-start.56 = (pred[32]{0:T(512)(128)(4,1)S(1)}, pred[32]{0:T(512)(128)(4,1)}, u32[]{:S(2)}) copy-start(pred[32]{0:T(512)(128)(4,1)} %copy-done.55) | copy-start | bytes 100
  112.9 8.3 %collective-permute-start.6 = (f32[1,6,32,128]{3,2,1,0:T(8,128)S(1)}, f32[1,6,32,128]{3,2,1,0:T(8,128)S(1)}, u32[]{:S(2)}, u32[]{:S(2)}) collective-permute-start(f32[1,6,32,128]{3,2,1,0:T(8,128)S(1)} %get-tuple-element.111), channel_id=1, source_target_pairs={{0,16},{16,32},{32,48},{48,64},{64,80},{80,96},{96,112},{112,128},... | collective-permute-start | bytes 294920 | tf_op jit(solution)/shard_map/ppermute | solution.py:28
  113.0 9.0 %collective-permute-start.5 = (f32[1,6,32,128]{3,2,1,0:T(8,128)S(1)}, f32[1,6,32,128]{3,2,1,0:T(8,128)S(1)}, u32[]{:S(2)}, u32[]{:S(2)}) collective-permute-start(f32[1,6,32,128]{3,2,1,0:T(8,128)S(1)} %get-tuple-element.110), channel_id=1, source_target_pairs={{16,0},{32,16},{48,32},{64,48},{80,64},{96,80},{112,96},{128,112},... | collective-permute-start | bytes 294920 | tf_op jit(solution)/shard_map/ppermute | solution.py:29
  123.6 1.2 copy-start.9
  123.6 1.3 %copy-start.10 = (f32[1,16,26,128]{3,2,1,0:T(8,128)S(1)}, f32[1,16,26,128]{3,2,1,0:T(8,128)}, u32[]{:S(2)}) copy-start(f32[1,16,26,128]{3,2,1,0:T(8,128)} %get-tuple-element.89) | copy-start | bytes 638980
  123.6 1.3 %copy-start.20 = (bf16[320,128,1]{1,0,2:T(8,128)(2,1)S(1)}, bf16[320,128,1]{1,0,2:T(8,128)(2,1)}, u32[]{:S(2)}) copy-start(bf16[320,128,1]{1,0,2:T(8,128)(2,1)} %reshape.2372) | copy-start | bytes 245764
  123.6 1.3 %copy-start.25 = (f32[1,16,5,128]{3,2,1,0:T(8,128)S(1)}, f32[1,16,5,128]{3,2,1,0:T(8,128)}, u32[]{:S(2)}) copy-start(f32[1,16,5,128]{3,2,1,0:T(8,128)} %get-tuple-element.90) | copy-start | bytes 122884
  123.6 1.3 %copy-start.26 = (f32[1,16,5,128]{3,2,1,0:T(8,128)S(1)}, f32[1,16,5,128]{3,2,1,0:T(8,128)}, u32[]{:S(2)}) copy-start(f32[1,16,5,128]{3,2,1,0:T(8,128)} %get-tuple-element.91) | copy-start | bytes 122884
  123.6 1.3 %copy-start.27 = (f32[1,16,6,128]{3,2,1,0:T(8,128)S(1)}, f32[1,16,6,128]{3,2,1,0:T(8,128)}, u32[]{:S(2)}) copy-start(f32[1,16,6,128]{3,2,1,0:T(8,128)} %get-tuple-element.86) | copy-start | bytes 147460
  123.7 1.3 %copy-start.28 = (f32[1,16,6,128]{3,2,1,0:T(8,128)S(1)}, f32[1,16,6,128]{3,2,1,0:T(8,128)}, u32[]{:S(2)}) copy-start(f32[1,16,6,128]{3,2,1,0:T(8,128)} %get-tuple-element.87) | copy-start | bytes 147460
  123.7 1.3 %copy-start.35 = (f32[1,16,3,128]{3,2,1,0:T(4,128)S(1)}, f32[1,16,3,128]{3,2,1,0:T(4,128)}, u32[]{:S(2)}) copy-start(f32[1,16,3,128]{3,2,1,0:T(4,128)} %get-tuple-element.99) | copy-start | bytes 73732
  123.7 1.3 %copy-start.36 = (f32[1,16,4,128]{3,2,1,0:T(4,128)S(1)}, f32[1,16,4,128]{3,2,1,0:T(4,128)}, u32[]{:S(2)}) copy-start(f32[1,16,4,128]{3,2,1,0:T(4,128)} %get-tuple-element.94) | copy-start | bytes 98308
  123.7 1.3 %copy-start.37 = (f32[1,16,4,128]{3,2,1,0:T(4,128)S(1)}, f32[1,16,4,128]{3,2,1,0:T(4,128)}, u32[]{:S(2)}) copy-start(f32[1,16,4,128]{3,2,1,0:T(4,128)} %get-tuple-element.95) | copy-start | bytes 98308
  123.7 1.3 copy-start.41
  123.7 1.3 copy-start.42
  123.7 1.3 copy-start.50
  123.7 1.3 copy-start.51
  123.7 1.3 copy-start.67
  123.7 1.4 %copy-start.70 = (f32[16,32,128]{2,1,0:T(8,128)S(1)}, f32[16,32,128]{2,1,0:T(8,128)}, u32[]{:S(2)}) copy-start(f32[16,32,128]{2,1,0:T(8,128)} %param.12) | copy-start | bytes 786436
  123.8 1.5 %copy-start.73 = (f32[1,16,32,128]{3,2,1,0:T(8,128)S(1)}, f32[1,16,32,128]{3,2,1,0:T(8,128)}, u32[]{:S(2)}) copy-start(f32[1,16,32,128]{3,2,1,0:T(8,128)} %get-tuple-element.166) | copy-start | bytes 786436
  (18 other events, 19.6 us)
